TPU v7x, 256 devices: a whole 4x4x8 slice. The times are simulated.
256 devices in a mesh: tensor: 32 (over x_hi, z, core), rows: 8 (over x_lo, y).
Axes of the slice: x: 4 (x_hi: 2, x_lo: 2; x = x_hi * 2 + x_lo), y: 4, z: 8, core: 2. Of those that a mesh axis runs over, the one named last changes fastest.
Arguments:
- image: bfloat16 [64, 64, 3072], P('rows', None, 'tensor'), may hold values from -6 to 6
- dw_kernel: bfloat16 [7, 7, 3072], P(None, None, 'tensor'), may hold values from -0.875 to 0.875
- dw_bias: float32 [3072], P('tensor'), may hold values from -3 to 3
- norm_gain: float32 [3072], replicated, may hold values from 0.1 to 1.9
- norm_bias: float32 [3072], replicated, may hold values from -2 to 2
- w_expand: bfloat16 [3072, 12288], P('rows', 'tensor'), may hold values from -0.21875 to 0.21875
- b_expand: float32 [12288], P('tensor'), may hold values from -3 to 3
- w_project: bfloat16 [12288, 3072], P('tensor', 'rows'), may hold values from -0.109375 to 0.109375
- b_project: float32 [3072], P('tensor'), may hold values from -3 to 3
- layer_scale: float32 [3072], P('tensor'), may hold values from 0.25 to 2
- out_grad: bfloat16 [64, 64, 3072], P('rows', None, 'tensor'), may hold values from -6 to 6
Outputs:
- result: bfloat16 [64, 64, 3072], P('rows', None, 'tensor')
- image_grad: bfloat16 [64, 64, 3072], P('rows', None, 'tensor')
- expand_grad: float32 [3072, 12288], P('rows', 'tensor')
- project_grad: float32 [12288, 3072], P('tensor', 'rows')
- kernel_grad: float32 [7, 7, 3072], P(None, None, 'tensor')
- scale_grad: float32 [3072], P('tensor')
All inputs are finite; a program needn't handle non-finite values.
Results may differ from a plain program's by a relative error of at most 0.022.
Values may be sent and summed in bfloat16 or wider, within the bound.
No kernel may reach another device: no remote copies, remote signals or barrier semaphores. Data moves between devices by JAX's collectives and lax.ppermute only.
A program may use at most 128 MiB of HBM per device.

v0:
```python
import math
import jax
import jax.numpy as jnp
from jax import lax
from jax.sharding import PartitionSpec as P

EPSILON = 1e-06


def extended(cells, sides, width):
    for axis, dim in sides:
        count = lax.axis_size(axis)
        ends = count - 1
        head = lax.slice_in_dim(cells, 0, width, axis=dim)
        tail = lax.slice_in_dim(cells, cells.shape[dim] - width, cells.shape[dim], axis=dim)
        cells = jnp.concatenate(
            [
                lax.ppermute(tail, axis, [(i, (i + 1) % count) for i in range(ends)]),
                cells,
                lax.ppermute(head, axis, [((i + 1) % count, i) for i in range(ends)]),
            ],
            axis=dim,
        )
    return cells


def gelu_exact(values):
    return 0.5 * values * (1.0 + lax.erf(values * (1.0 / math.sqrt(2.0))))


def gelu_slope(values):
    cumulative = 0.5 * (1.0 + lax.erf(values * (1.0 / math.sqrt(2.0))))
    density = jnp.exp(-0.5 * values * values) * (1.0 / math.sqrt(2.0 * math.pi))
    return cumulative + values * density


def depthwise(padded, kernel, height, breadth):
    kernel_size = kernel.shape[0]
    summed = jnp.zeros((height, breadth, kernel.shape[2]), jnp.float32)
    for row_shift in range(kernel_size):
        for col_shift in range(kernel_size):
            window = padded[row_shift : row_shift + height, col_shift : col_shift + breadth]
            summed = summed + kernel[row_shift, col_shift].astype(jnp.float32) * window
    return summed


def kernel_terms(padded, gradient, kernel_size):
    height, breadth = (gradient.shape[0], gradient.shape[1])
    kernel_rows = []
    for row_shift in range(kernel_size):
        kernel_line = []
        for col_shift in range(kernel_size):
            window = padded[row_shift : row_shift + height, col_shift : col_shift + breadth]
            kernel_line.append(jnp.sum(window * gradient, axis=(0, 1)))
        kernel_rows.append(jnp.stack(kernel_line))
    return jnp.stack(kernel_rows)


def contract_last(left, right):
    return lax.dot_general(
        left, right, (((1,), (1,)), ((), ())), preferred_element_type=jnp.float32
    )


def contract_first(left, right):
    return lax.dot_general(
        left, right, (((0,), (0,)), ((), ())), preferred_element_type=jnp.float32
    )


def per_device(
    image,
    dw_kernel,
    dw_bias,
    norm_gain,
    norm_bias,
    w_expand,
    b_expand,
    w_project,
    b_project,
    layer_scale,
    out_grad,
):
    kernel_size = dw_kernel.shape[0]
    rim_depth = kernel_size // 2
    height, breadth, channels = image.shape
    positions = height * breadth
    features = norm_gain.shape[0]
    channel_start = lax.axis_index("tensor") * channels
    gain_part = lax.dynamic_slice_in_dim(norm_gain, channel_start, channels)
    shift_part = lax.dynamic_slice_in_dim(norm_bias, channel_start, channels)
    rimmed = extended(image, (("rows", 0),), rim_depth)
    wide_image = jnp.pad(rimmed, ((0, 0), (rim_depth, rim_depth), (0, 0))).astype(jnp.float32)
    convolved = depthwise(wide_image, dw_kernel, height, breadth) + dw_bias
    mixed = convolved.astype(jnp.bfloat16).reshape(positions, channels)
    own_mixed = mixed.astype(jnp.float32)
    plain_sum, square_sum = lax.psum(
        (jnp.sum(own_mixed, 1), jnp.sum(own_mixed * own_mixed, 1)), "tensor"
    )
    average = plain_sum[:, None] / features
    inv_std = lax.rsqrt(square_sum[:, None] / features - average * average + EPSILON)
    centred = (own_mixed - average) * inv_std
    normed_part = (centred * gain_part + shift_part).astype(jnp.bfloat16)
    normed = lax.all_gather(normed_part, "tensor", axis=1, tiled=True)
    columns = normed
    pre = jnp.dot(
        columns,
        lax.all_gather(w_expand, "rows", axis=0, tiled=True),
        preferred_element_type=jnp.float32,
    )
    pre = pre + b_expand
    hidden = gelu_exact(pre).astype(jnp.bfloat16)
    partial_out = jnp.dot(
        hidden,
        lax.all_gather(w_project, "rows", axis=1, tiled=True),
        preferred_element_type=jnp.float32,
    )
    projected = (
        lax.psum_scatter(
            partial_out.astype(jnp.bfloat16), "tensor", scatter_dimension=1, tiled=True
        ).astype(jnp.float32)
        + b_project
    )
    residual = image.reshape(positions, channels).astype(jnp.float32)
    result = (
        (residual + layer_scale * projected).astype(jnp.bfloat16).reshape(height, breadth, channels)
    )
    upstream = out_grad.reshape(positions, channels).astype(jnp.float32)
    scale_term = jnp.sum(upstream * projected, 0)
    scaled_grad = (upstream * layer_scale).astype(jnp.bfloat16)
    grad_panels = lax.all_gather(scaled_grad, "tensor", axis=1, tiled=True)
    project_term = contract_first(hidden, grad_panels)
    project_grad = lax.psum_scatter(
        project_term.astype(jnp.bfloat16), "rows", scatter_dimension=1, tiled=True
    ).astype(jnp.float32)
    columns = grad_panels
    hidden_grad = contract_last(columns, lax.all_gather(w_project, "rows", axis=1, tiled=True))
    pre_grad = (hidden_grad * gelu_slope(pre)).astype(jnp.bfloat16)
    columns = normed
    expand_grad = lax.psum_scatter(
        contract_first(columns, pre_grad).astype(jnp.bfloat16),
        "rows",
        scatter_dimension=0,
        tiled=True,
    ).astype(jnp.float32)
    normed_partial = contract_last(pre_grad, lax.all_gather(w_expand, "rows", axis=0, tiled=True))
    normed_grad = lax.psum_scatter(
        normed_partial.astype(jnp.bfloat16), "tensor", scatter_dimension=1, tiled=True
    ).astype(jnp.float32)
    gain_grad = normed_grad * gain_part
    plain_total, centred_total = lax.psum(
        (jnp.sum(gain_grad, 1), jnp.sum(gain_grad * centred, 1)), "tensor"
    )
    plain_mean = plain_total[:, None] / features
    centred_mean = centred_total[:, None] / features
    mixed_grad = (inv_std * (gain_grad - plain_mean - centred * centred_mean)).astype(jnp.bfloat16)
    mixed_grad = mixed_grad.reshape(height, breadth, channels)
    grad_rimmed = extended(mixed_grad, (("rows", 0),), rim_depth)
    wide_grad = jnp.pad(grad_rimmed, ((0, 0), (rim_depth, rim_depth), (0, 0))).astype(jnp.float32)
    back = depthwise(wide_grad, dw_kernel[::-1, ::-1], height, breadth)
    image_grad = (upstream.reshape(height, breadth, channels) + back).astype(jnp.bfloat16)
    kernel_local = kernel_terms(wide_image, mixed_grad.astype(jnp.float32), kernel_size)
    kernel_grad, scale_grad = lax.psum((kernel_local, scale_term), "rows")
    return (result, image_grad, expand_grad, project_grad, kernel_grad, scale_grad)


def solution(mesh):
    return jax.shard_map(
        per_device,
        mesh=mesh,
        in_specs=(
            P("rows", None, "tensor"),
            P(None, None, "tensor"),
            P("tensor"),
            P(),
            P(),
            P("rows", "tensor"),
            P("tensor"),
            P("tensor", "rows"),
            P("tensor"),
            P("tensor"),
            P("rows", None, "tensor"),
        ),
        out_specs=(
            P("rows", None, "tensor"),
            P("rows", None, "tensor"),
            P("rows", "tensor"),
            P("tensor", "rows"),
            P(None, None, "tensor"),
            P("tensor"),
        ),
        check_vma=False,
    )
```

profile of v0, /device:TPU:38, one launch (start us, length us, event | category | flops | bytes accessed | tf_op | source)
XLA Modules:
  0.0 697.6 jit_solution(9709800327366942939)
XLA Ops:
  8.8 3.5 collective-permute-start
  12.3 4.5 collective-permute-start.1
  22.2 2.7 convert_reduce_fusion
  25.1 65.2 %all-reduce.3 = (f32[512]{0:T(512)S(1)}, f32[512]{0:T(512)S(1)}) all-reduce(f32[512]{0:T(512)S(1)} %reduce_sum.493, f32[512]{0:T(512)S(1)} %reduce_sum.491), channel_id=1, replica_groups=mesh['tensor'=32,'rows'=8] {'tensor'}, use_global_device_ids=true, to_apply=%region_3.4 | all-reduce | flops 1024 | bytes 8192 | tf_op jit(solution)/shard_map/psum | solution.py:97
  91.9 79.8 %all-gather.5.cloned.1.call-done = bf16[512,3072]{0,1:T(8,128)(2,1)} async-done(((bf16[512,96]{0,1:T(8,128)(2,1)}), bf16[512,3072]{0,1:T(8,128)(2,1)}) %all-gather.5.cloned.1.call-update) | async-done | bytes 3145744 | tf_op jit(solution)/shard_map/all_gather | solution.py:104
  171.7 4.5 convolution_add_fusion
  176.2 40.6 %all-gather.9.cloned.1.call-done = bf16[384,3072]{1,0:T(8,128)(2,1)} async-done(((bf16[384,384]{1,0:T(8,128)(2,1)}), bf16[384,3072]{1,0:T(8,128)(2,1)}) %all-gather.9.cloned.1.call-update) | async-done | bytes 2359312 | tf_op jit(solution)/shard_map/all_gather | solution.py:115
  216.8 5.3 convolution_convert_fusion.1
  223.3 120.4 %reduce-scatter.7.cloned.1.call-done = bf16[512,96]{0,1:T(8,128)(2,1)} async-done(((bf16[512,3072]{0,1:T(8,128)(2,1)}), bf16[512,96]{0,1:T(8,128)(2,1)}) %reduce-scatter.7.cloned.1.call-update) | async-done | bytes 98320 | tf_op jit(solution)/shard_map/reduce_scatter | solution.py:119
  343.7 1.8 multiply_reduce_fusion.1
  345.6 82.8 %all-gather.11.cloned.1.call-done = bf16[512,3072]{0,1:T(8,128)(2,1)} async-done(((bf16[512,96]{0,1:T(8,128)(2,1)}), bf16[512,3072]{0,1:T(8,128)(2,1)}) %all-gather.11.cloned.1.call-update) | async-done | bytes 3145744 | tf_op jit(solution)/shard_map/all_gather | solution.py:131
  428.4 4.7 fusion
  433.9 3.5 convolution_convert_fusion
  437.7 3.6 convolution_convert_fusion.2
  441.3 2.5 copy.41
  443.8 5.2 convolution_convert_fusion.3
  449.8 108.2 %reduce-scatter.9.cloned.1.call-done = bf16[512,96]{0,1:T(8,128)(2,1)} async-done(((bf16[512,3072]{0,1:T(8,128)(2,1)}), bf16[512,96]{0,1:T(8,128)(2,1)}) %reduce-scatter.9.cloned.1.call-update) | async-done | bytes 98320 | tf_op jit(solution)/shard_map/reduce_scatter | solution.py:147
  558.9 60.7 %all-reduce.2 = (f32[512]{0:T(512)S(1)}, f32[512]{0:T(512)S(1)}) all-reduce(f32[512]{0:T(512)S(1)} %get-tuple-element.64, f32[512]{0:T(512)S(1)} %get-tuple-element.63), channel_id=1, replica_groups=mesh['tensor'=32,'rows'=8] {'tensor'}, use_global_device_ids=true, to_apply=%region_9.10 | all-reduce | flops 1024 | bytes 8192 | tf_op jit(solution)/shard_map/psum | solution.py:151
  621.1 5.2 collective-permute-start.3
  626.3 1.9 collective-permute-start.2
  632.3 22.2 %reduce-scatter.11.cloned.1.call-done = bf16[384,384]{1,0:T(8,128)(2,1)} async-done(((bf16[3072,384]{1,0:T(8,128)(2,1)}), bf16[384,384]{1,0:T(8,128)(2,1)}) %reduce-scatter.11.cloned.1.call-update) | async-done | bytes 294928 | tf_op jit(solution)/shard_map/reduce_scatter | solution.py:140
  654.5 1.8 convert_element_type.304
  656.3 32.2 %all-reduce.4 = (f32[7,7,96]{2,1,0:T(8,128)}, f32[96]{0:T(128)}) all-reduce(f32[7,7,96]{2,1,0:T(8,128)S(1)} %constant_dynamic-update-slice_fusion, f32[96]{0:T(128)S(1)} %get-tuple-element.72), channel_id=1, replica_groups=mesh['tensor'=32,'rows'=8] {'rows'}, use_global_device_ids=true, to_apply=%region_61.62 | all-reduce | flops 4800 | bytes 38400 | tf_op jit(solution)/shard_map/psum | solution.py:163
  688.6 2.2 fusion.57
  (81 shorter events, 18.3 us)
Async XLA Ops:
  7.2 84.7 %all-gather.7.cloned.1.call-start = ((), (), s32[]{:S(2)}) async-start(), calls=%async_computation.5 | async-start | bytes 2654208 | tf_op jit(solution)/shard_map/all_gather | solution.py:108
  7.9 163.8 %all-gather.5.cloned.1.call-start = ((), (), s32[]{:S(2)}) async-start(), calls=%async_computation.4 | async-start | bytes 3244032 | tf_op jit(solution)/shard_map/all_gather | solution.py:104
  8.8 12.4 %collective-permute-start = (bf16[3,64,96]{2,1,0:T(8,128)(2,1)S(1)}, bf16[3,64,96]{2,1,0:T(8,128)(2,1)S(1)}, u32[]{:S(2)}, u32[]{:S(2)}) collective-permute-start(bf16[3,64,96]{2,1,0:T(8,128)(2,1)S(1)} %get-tuple-element.74), channel_id=1, source_target_pairs={{0,1},{1,2},{2,3},{3,4},{4,5},{5,6},{6,7},{8,9},{9,10},{10,11},{11... | collective-permute-start | bytes 110600 | tf_op jit(solution)/shard_map/ppermute | solution.py:18
  12.3 8.9 %collective-permute-start.1 = (bf16[3,64,96]{2,1,0:T(8,128)(2,1)S(1)}, bf16[3,64,96]{2,1,0:T(8,128)(2,1)S(1)}, u32[]{:S(2)}, u32[]{:S(2)}) collective-permute-start(bf16[3,64,96]{2,1,0:T(8,128)(2,1)S(1)} %get-tuple-element.75), channel_id=1, source_target_pairs={{1,0},{2,1},{3,2},{4,3},{5,4},{6,5},{7,6},{9,8},{10,9},{11,10},{12... | collective-permute-start | bytes 110600 | tf_op jit(solution)/shard_map/ppermute | solution.py:20
  22.2 149.6 %copy-start.5 = (f32[384]{0:T(512)S(1)}, f32[384]{0:T(512)}, u32[]{:S(2)}) copy-start(f32[384]{0:T(512)} %param.17) | copy-start | bytes 4612
  91.1 125.7 %all-gather.9.cloned.1.call-start = ((), (), s32[]{:S(2)}) async-start(), calls=%async_computation.6 | async-start | bytes 2654208 | tf_op jit(solution)/shard_map/all_gather | solution.py:115
  91.8 251.9 %reduce-scatter.7.cloned.1.call-start = ((), (), s32[]{:S(2)}) async-start(), calls=%async_computation.7 | async-start | bytes 3244032 | tf_op jit(solution)/shard_map/reduce_scatter | solution.py:119
  176.2 40.7 %copy-start.6 = (f32[512,384]{1,0:T(8,128)}, f32[512,384]{1,0:T(8,128)S(1)}, u32[]{:S(2)}) copy-start(f32[512,384]{1,0:T(8,128)S(1)} %convolution_add_fusion) | copy-start | bytes 2359300
  222.1 0.9 copy-start.1
  222.1 1.0 copy-start
  222.1 121.6 %copy-start.2 = (f32[96]{0:T(128)S(1)}, f32[96]{0:T(128)}, u32[]{:S(2)}) copy-start(f32[96]{0:T(128)} %param.19) | copy-start | bytes 1156
  222.1 121.6 %copy-start.3 = (f32[96]{0:T(128)S(1)}, f32[96]{0:T(128)}, u32[]{:S(2)}) copy-start(f32[96]{0:T(128)} %param.20) | copy-start | bytes 1156
  222.1 206.2 %all-gather.11.cloned.1.call-start = ((), (), s32[]{:S(2)}) async-start(), calls=%async_computation.8 | async-start | bytes 3244032 | tf_op jit(solution)/shard_map/all_gather | solution.py:131
  345.5 88.4 %copy-start.4 = (bf16[3072,384]{1,0:T(8,128)(2,1)S(1)}, bf16[3072,384]{1,0:T(8,128)(2,1)}, u32[]{:S(2)}) copy-start(bf16[3072,384]{1,0:T(8,128)(2,1)} %all-gather.7.cloned.1.call-done) | copy-start | bytes 7077892
  345.5 212.4 %reduce-scatter.9.cloned.1.call-start = ((), (), s32[]{:S(2)}) async-start(), calls=%async_computation.9 | async-start | bytes 3244032 | tf_op jit(solution)/shard_map/reduce_scatter | solution.py:147
  433.1 0.7 copy-start.7
  437.4 192.8 %reduce-scatter.13.cloned.1.call-start = ((), (), s32[]{:S(2)}) async-start(), calls=%async_computation.11 | async-start | bytes 2654208
  443.7 210.7 %reduce-scatter.11.cloned.1.call-start = ((), (), s32[]{:S(2)}) async-start(), calls=%async_computation.10 | async-start | bytes 2654208 | tf_op jit(solution)/shard_map/reduce_scatter | solution.py:140
  621.1 67.4 %collective-permute-start.3 = (bf16[3,64,96]{2,1,0:T(8,128)(2,1)S(1)}, bf16[3,64,96]{2,1,0:T(8,128)(2,1)S(1)}, u32[]{:S(2)}, u32[]{:S(2)}) collective-permute-start(bf16[3,64,96]{2,1,0:T(8,128)(2,1)S(1)} %bitcast.289), channel_id=1, source_target_pairs={{1,0},{2,1},{3,2},{4,3},{5,4},{6,5},{7,6},{9,8},{10,9},{11,10},{12... | collective-permute-start | bytes 110600 | tf_op jit(solution)/shard_map/ppermute | solution.py:20
  626.3 62.2 %collective-permute-start.2 = (bf16[3,64,96]{2,1,0:T(8,128)(2,1)S(1)}, bf16[3,64,96]{2,1,0:T(8,128)(2,1)S(1)}, u32[]{:S(2)}, u32[]{:S(2)}) collective-permute-start(bf16[3,64,96]{2,1,0:T(8,128)(2,1)S(1)} %bitcast.288), channel_id=1, source_target_pairs={{0,1},{1,2},{2,3},{3,4},{4,5},{5,6},{6,7},{8,9},{9,10},{10,11},{11... | collective-permute-start | bytes 110600 | tf_op jit(solution)/shard_map/ppermute | solution.py:18
Sparse Core Ops, SparseCore 0:
  9.8 46.1 all-gather.6
  91.2 80.4 all-gather.4
  173.5 43.2 all-gather.8
  222.3 121.3 reduce-scatter.6
  347.3 81.0 all-gather.10
  437.5 120.3 reduce-scatter.8
  560.5 45.4 reduce-scatter.12
  608.6 45.8 reduce-scatter.10
where the time goes:
time: 698 us
  waiting for transfers between devices  456 us (65%)
  blocking collectives  158 us (23%)
  matrix products  26.7 us (4%)
  other arithmetic  17.7 us (3%)
  starting transfers between devices  15.6 us (2%)
  between operations  14.4 us (2%)
  local copies, waits for them, and re-layouts  9.46 us (1%)
    reduce_scatter x1, waiting for transfers between devices, per_device(): lax.psum_scatter(partial_out.astype(jnp.bfloat16), 'tensor', scatter_dime...  120 us
    reduce_scatter x1, waiting for transfers between devices, per_device(): lax.psum_scatter(normed_partial.astype(jnp.bfloat16), 'tensor', scatter_d...  108 us
    all_gather x1, waiting for transfers between devices, per_device(): grad_panels = lax.all_gather(scaled_grad, 'tensor', axis=1, tiled=True)  82.8 us
    all_gather x1, waiting for transfers between devices, per_device(): normed = lax.all_gather(normed_part, 'tensor', axis=1, tiled=True)  79.8 us
    psum x1, blocking collectives, per_device(): lax.psum((jnp.sum(own_mixed, 1), jnp.sum(own_mixed * own_mixed, 1)), 'ten...  65.2 us
    psum x1, blocking collectives, per_device(): lax.psum((jnp.sum(gain_grad, 1), jnp.sum(gain_grad * centred, 1)), 'tensor')  60.7 us
    all_gather x1, waiting for transfers between devices, per_device(): lax.all_gather(w_project, 'rows', axis=1, tiled=True)  40.6 us
    psum x1, blocking collectives, per_device(): kernel_grad, scale_grad = lax.psum((kernel_local, scale_term), 'rows')  32.2 us
  transfers between devices with their start and end apart: 12, of which 6 were waited for; matrix products, arithmetic and copies ran while one was open for 5% of the time, Pallas kernels for 0%

commit v1 on v0

--- a/solution.py
+++ b/solution.py
@@ -101,7 +101,9 @@
     inv_std = lax.rsqrt(square_sum[:, None] / features - average * average + EPSILON)
     centred = (own_mixed - average) * inv_std
     normed_part = (centred * gain_part + shift_part).astype(jnp.bfloat16)
-    normed = lax.all_gather(normed_part, "tensor", axis=1, tiled=True)
+    normed = jnp.concatenate(
+        lax.all_to_all(jnp.stack([normed_part] * lax.axis_size("tensor")), "tensor", 0, 0), axis=1
+    )
     columns = normed
     pre = jnp.dot(
         columns,

time: 698 us -> 661 us (0.947)
  waiting for transfers between devices: 456 us -> 404 us
  starting transfers between devices: 15.6 us -> 27.5 us
    all_gather x1 -> x0, waiting for transfers between devices: 79.8 us -> none  [per_device(): normed = lax.all_gather(normed_part, 'tensor', axis=1, tiled=True)]
    all_to_all x0 -> x1, waiting for transfers between devices: none -> 69.4 us  [per_device(): lax.all_to_all(jnp.stack([normed_part] * lax.axis_size('tensor')), 'tenso...]
    all_gather x1, waiting for transfers between devices: 40.6 us -> 0.02 us  [per_device(): lax.all_gather(w_project, 'rows', axis=1, tiled=True)]
    all_to_all x0 -> x1, starting transfers between devices: none -> 12.1 us  [per_device(): lax.all_to_all(jnp.stack([normed_part] * lax.axis_size('tensor')), 'tenso...]
  transfers between devices with their start and end apart: 12 -> 12, of which waited for: 6 -> 5; matrix products, arithmetic and copies ran while one was open for 5% -> 5% of each run, Pallas kernels for 0% -> 0%
where the time goes in v1:
time: 661 us; the launch traced here: 660 us
  waiting for transfers between devices  404 us (61%)
  blocking collectives  159 us (24%)
  starting transfers between devices  27.5 us (4%)
  matrix products  26.8 us (4%)
  other arithmetic  17 us (3%)
  between operations  14.4 us (2%)
  local copies, waits for them, and re-layouts  12.4 us (2%)
    reduce_scatter x1, waiting for transfers between devices, per_device(): lax.psum_scatter(partial_out.astype(jnp.bfloat16), 'tensor', scatter_dime...  120 us
    reduce_scatter x1, waiting for transfers between devices, per_device(): lax.psum_scatter(normed_partial.astype(jnp.bfloat16), 'tensor', scatter_d...  108 us
    all_gather x1, waiting for transfers between devices, per_device(): grad_panels = lax.all_gather(scaled_grad, 'tensor', axis=1, tiled=True)  82.7 us
    all_to_all x1, waiting for transfers between devices, per_device(): lax.all_to_all(jnp.stack([normed_part] * lax.axis_size('tensor')), 'tenso...  69.4 us
    psum x1, blocking collectives, per_device(): lax.psum((jnp.sum(own_mixed, 1), jnp.sum(own_mixed * own_mixed, 1)), 'ten...  65.2 us
    psum x1, blocking collectives, per_device(): lax.psum((jnp.sum(gain_grad, 1), jnp.sum(gain_grad * centred, 1)), 'tensor')  60.7 us
    psum x1, blocking collectives, per_device(): kernel_grad, scale_grad = lax.psum((kernel_local, scale_term), 'rows')  32.6 us
    reduce_scatter x1, waiting for transfers between devices, per_device(): lax.psum_scatter(contract_first(columns, pre_grad).astype(jnp.bfloat16),...  21.7 us
  transfers between devices with their start and end apart: 12, of which 5 were waited for; matrix products, arithmetic and copies ran while one was open for 5% of the time, Pallas kernels for 0%

profile of v1, /device:TPU:38, one launch (start us, length us, event | category | flops | bytes accessed | tf_op | source)
XLA Modules:
  0.0 660.3 jit_solution(5477954143671447938)
XLA Ops:
  8.7 3.5 collective-permute-start
  12.2 4.5 collective-permute-start.1
  22.1 2.6 convert_reduce_fusion
  25.0 65.2 %all-reduce.3 = (f32[512]{0:T(512)S(1)}, f32[512]{0:T(512)S(1)}) all-reduce(f32[512]{0:T(512)S(1)} %reduce_sum.493, f32[512]{0:T(512)S(1)} %reduce_sum.491), channel_id=1, replica_groups=mesh['tensor'=32,'rows'=8] {'tensor'}, use_global_device_ids=true, to_apply=%region_3.4 | all-reduce | flops 1024 | bytes 8192 | tf_op jit(solution)/shard_map/psum | solution.py:97
  90.4 2.1 stack.227
  92.4 12.1 %all-to-all-start = ((bf16[32,512,96]{1,2,0:T(8,128)(2,1)}), bf16[32,512,96]{1,2,0:T(8,128)(2,1)}, u32[]{:S(2)}, u32[]{:S(2)}) async-start(bf16[32,512,96]{1,2,0:T(8,128)(2,1)} %stack.227), calls=%async_computation | async-start | bytes 6291456 | tf_op jit(solution)/shard_map/all_to_all | solution.py:105
  105.3 69.4 %all-to-all-done = bf16[32,512,96]{1,2,0:T(8,128)(2,1)} async-done(((bf16[32,512,96]{1,2,0:T(8,128)(2,1)}), bf16[32,512,96]{1,2,0:T(8,128)(2,1)}, u32[]{:S(2)}, u32[]{:S(2)}) %all-to-all-start) | async-done | bytes 3145760 | tf_op jit(solution)/shard_map/all_to_all | solution.py:105
  174.8 4.5 convolution_add_fusion
  180.2 5.3 convolution_convert_fusion.1
  186.6 120.2 %reduce-scatter.7.cloned.1.call-done = bf16[512,96]{0,1:T(8,128)(2,1)} async-done(((bf16[512,3072]{0,1:T(8,128)(2,1)}), bf16[512,96]{0,1:T(8,128)(2,1)}) %reduce-scatter.7.cloned.1.call-update) | async-done | bytes 98320 | tf_op jit(solution)/shard_map/reduce_scatter | solution.py:121
  308.7 82.7 %all-gather.8.cloned.1.call-done = bf16[512,3072]{0,1:T(8,128)(2,1)} async-done(((bf16[512,96]{0,1:T(8,128)(2,1)}), bf16[512,3072]{0,1:T(8,128)(2,1)}) %all-gather.8.cloned.1.call-update) | async-done | bytes 3145744 | tf_op jit(solution)/shard_map/all_gather | solution.py:133
  391.4 4.7 fusion
  396.9 3.6 convolution_convert_fusion
  400.7 3.6 convolution_convert_fusion.2
  404.3 2.5 copy.42
  406.8 5.2 convolution_convert_fusion.3
  412.8 108.1 %reduce-scatter.9.cloned.1.call-done = bf16[512,96]{0,1:T(8,128)(2,1)} async-done(((bf16[512,3072]{0,1:T(8,128)(2,1)}), bf16[512,96]{0,1:T(8,128)(2,1)}) %reduce-scatter.9.cloned.1.call-update) | async-done | bytes 98320 | tf_op jit(solution)/shard_map/reduce_scatter | solution.py:149
  521.9 60.7 %all-reduce.2 = (f32[512]{0:T(512)S(1)}, f32[512]{0:T(512)S(1)}) all-reduce(f32[512]{0:T(512)S(1)} %get-tuple-element.64, f32[512]{0:T(512)S(1)} %get-tuple-element.63), channel_id=1, replica_groups=mesh['tensor'=32,'rows'=8] {'tensor'}, use_global_device_ids=true, to_apply=%region_9.10 | all-reduce | flops 1024 | bytes 8192 | tf_op jit(solution)/shard_map/psum | solution.py:153
  584.1 5.1 collective-permute-start.3
  589.2 1.9 collective-permute-start.2
  595.2 21.7 %reduce-scatter.11.cloned.1.call-done = bf16[384,384]{1,0:T(8,128)(2,1)} async-done(((bf16[3072,384]{1,0:T(8,128)(2,1)}), bf16[384,384]{1,0:T(8,128)(2,1)}) %reduce-scatter.11.cloned.1.call-update) | async-done | bytes 294928 | tf_op jit(solution)/shard_map/reduce_scatter | solution.py:142
  616.9 1.8 convert_element_type.308
  618.7 32.6 %all-reduce.4 = (f32[7,7,96]{2,1,0:T(8,128)}, f32[96]{0:T(128)}) all-reduce(f32[7,7,96]{2,1,0:T(8,128)S(1)} %constant_dynamic-update-slice_fusion, f32[96]{0:T(128)S(1)} %get-tuple-element.72), channel_id=1, replica_groups=mesh['tensor'=32,'rows'=8] {'rows'}, use_global_device_ids=true, to_apply=%region_61.62 | all-reduce | flops 4800 | bytes 38400 | tf_op jit(solution)/shard_map/psum | solution.py:165
  651.3 2.2 fusion.57
  (81 shorter events, 20.3 us)
Async XLA Ops:
  7.2 98.2 %all-gather.4.cloned.1.call-start = ((), (), s32[]{:S(2)}) async-start(), calls=%async_computation.5 | async-start | bytes 2654208 | tf_op jit(solution)/shard_map/all_gather | solution.py:110
  8.7 12.4 %collective-permute-start = (bf16[3,64,96]{2,1,0:T(8,128)(2,1)S(1)}, bf16[3,64,96]{2,1,0:T(8,128)(2,1)S(1)}, u32[]{:S(2)}, u32[]{:S(2)}) collective-permute-start(bf16[3,64,96]{2,1,0:T(8,128)(2,1)S(1)} %get-tuple-element.74), channel_id=1, source_target_pairs={{0,1},{1,2},{2,3},{3,4},{4,5},{5,6},{6,7},{8,9},{9,10},{10,11},{11... | collective-permute-start | bytes 110600 | tf_op jit(solution)/shard_map/ppermute | solution.py:18
  12.2 8.9 %collective-permute-start.1 = (bf16[3,64,96]{2,1,0:T(8,128)(2,1)S(1)}, bf16[3,64,96]{2,1,0:T(8,128)(2,1)S(1)}, u32[]{:S(2)}, u32[]{:S(2)}) collective-permute-start(bf16[3,64,96]{2,1,0:T(8,128)(2,1)S(1)} %get-tuple-element.75), channel_id=1, source_target_pairs={{1,0},{2,1},{3,2},{4,3},{5,4},{6,5},{7,6},{9,8},{10,9},{11,10},{12... | collective-permute-start | bytes 110600 | tf_op jit(solution)/shard_map/ppermute | solution.py:20
  92.4 82.3 %copy-start.5 = (f32[384]{0:T(512)S(1)}, f32[384]{0:T(512)}, u32[]{:S(2)}) copy-start(f32[384]{0:T(512)} %param.17) | copy-start | bytes 4612
  92.4 82.3 %all-to-all-start = ((bf16[32,512,96]{1,2,0:T(8,128)(2,1)}), bf16[32,512,96]{1,2,0:T(8,128)(2,1)}, u32[]{:S(2)}, u32[]{:S(2)}) async-start(bf16[32,512,96]{1,2,0:T(8,128)(2,1)} %stack.227), calls=%async_computation | async-start | bytes 6291456 | tf_op jit(solution)/shard_map/all_to_all | solution.py:105
  104.5 74.8 %all-gather.6.cloned.1.call-start = ((), (), s32[]{:S(2)}) async-start(), calls=%async_computation.6 | async-start | bytes 2654208 | tf_op jit(solution)/shard_map/all_gather | solution.py:117
  105.3 201.6 %reduce-scatter.7.cloned.1.call-start = ((), (), s32[]{:S(2)}) async-start(), calls=%async_computation.7 | async-start | bytes 3244032 | tf_op jit(solution)/shard_map/reduce_scatter | solution.py:121
  179.2 0.9 copy-start.6
  185.4 0.9 copy-start.1
  185.4 1.0 copy-start
  185.4 121.4 %copy-start.2 = (f32[96]{0:T(128)S(1)}, f32[96]{0:T(128)}, u32[]{:S(2)}) copy-start(f32[96]{0:T(128)} %param.19) | copy-start | bytes 1156
  185.4 121.4 %copy-start.3 = (f32[96]{0:T(128)S(1)}, f32[96]{0:T(128)}, u32[]{:S(2)}) copy-start(f32[96]{0:T(128)} %param.20) | copy-start | bytes 1156
  185.5 205.9 %all-gather.8.cloned.1.call-start = ((), (), s32[]{:S(2)}) async-start(), calls=%async_computation.8 | async-start | bytes 3244032 | tf_op jit(solution)/shard_map/all_gather | solution.py:133
  308.6 88.3 %copy-start.4 = (bf16[3072,384]{1,0:T(8,128)(2,1)S(1)}, bf16[3072,384]{1,0:T(8,128)(2,1)}, u32[]{:S(2)}) copy-start(bf16[3072,384]{1,0:T(8,128)(2,1)} %all-gather.4.cloned.1.call-done) | copy-start | bytes 7077892
  308.6 212.3 %reduce-scatter.9.cloned.1.call-start = ((), (), s32[]{:S(2)}) async-start(), calls=%async_computation.9 | async-start | bytes 3244032 | tf_op jit(solution)/shard_map/reduce_scatter | solution.py:149
  396.1 0.7 copy-start.7
  400.4 192.7 %reduce-scatter.13.cloned.1.call-start = ((), (), s32[]{:S(2)}) async-start(), calls=%async_computation.11 | async-start | bytes 2654208
  406.8 210.1 %reduce-scatter.11.cloned.1.call-start = ((), (), s32[]{:S(2)}) async-start(), calls=%async_computation.10 | async-start | bytes 2654208 | tf_op jit(solution)/shard_map/reduce_scatter | solution.py:142
  584.1 67.1 %collective-permute-start.3 = (bf16[3,64,96]{2,1,0:T(8,128)(2,1)S(1)}, bf16[3,64,96]{2,1,0:T(8,128)(2,1)S(1)}, u32[]{:S(2)}, u32[]{:S(2)}) collective-permute-start(bf16[3,64,96]{2,1,0:T(8,128)(2,1)S(1)} %bitcast.292), channel_id=1, source_target_pairs={{1,0},{2,1},{3,2},{4,3},{5,4},{6,5},{7,6},{9,8},{10,9},{11,10},{12... | collective-permute-start | bytes 110600 | tf_op jit(solution)/shard_map/ppermute | solution.py:20
  589.2 62.0 %collective-permute-start.2 = (bf16[3,64,96]{2,1,0:T(8,128)(2,1)S(1)}, bf16[3,64,96]{2,1,0:T(8,128)(2,1)S(1)}, u32[]{:S(2)}, u32[]{:S(2)}) collective-permute-start(bf16[3,64,96]{2,1,0:T(8,128)(2,1)S(1)} %bitcast.291), channel_id=1, source_target_pairs={{0,1},{1,2},{2,3},{3,4},{4,5},{5,6},{6,7},{8,9},{9,10},{10,11},{11... | collective-permute-start | bytes 110600 | tf_op jit(solution)/shard_map/ppermute | solution.py:18
Sparse Core Ops, SparseCore 0:
  9.8 46.1 all-gather.3
  107.1 58.6 all-gather.5
  185.6 121.1 reduce-scatter.6
  310.4 80.9 all-gather.7
  400.6 120.3 reduce-scatter.8
  523.4 45.4 reduce-scatter.12
  571.4 45.3 reduce-scatter.10
